TPU v7x, 512 devices: a whole 4x8x8 slice. The times are simulated.
512 devices in a mesh: tm: 16 (over z, y_hi), space: 32 (over x, y_lo, core).
Axes of the slice: x: 4, y: 8 (y_hi: 2, y_lo: 4; y = y_hi * 4 + y_lo), z: 8, core: 2. Of those that a mesh axis runs over, the one named last changes fastest.
Arguments:
- state: float32 [16, 5, 256, 32, 128], P('tm', None, 'space'), may hold values from -6 to 6
- base: float32 [16, 5, 256, 32, 128], P('tm', None, 'space'), may hold values from -6 to 6
- pseudo_step: float32 [256, 32, 128], P('space'), may hold values from 0.05 to 0.3
- eddy_visc: float32 [256, 32, 128], P('space'), may hold values from 0.02 to 0.2
- jacobians: float32 [3, 5, 5], replicated, may hold values from -2.5 to 2.5
- partner_radial: int32 [2, 256, 128], P(None, 'space'), may hold values from 0 to 127, each once within a row
- partner_instance: int32 [16, 2, 256, 128], P('tm', None, 'space'), may hold values from 0 to 15, as said below
Outputs:
- updated: float32 [16, 5, 256, 32, 128], P('tm', None, 'space')
Inputs may be any that keep to these rules, and one draw needn't show every extreme that they name: partner_radial[s, i, :] is a permutation of the radial indices 0..127: the partner cells on the opposite periodic face in the same axial plane. partner_instance[n, 0, i, k] = (n + L_i) mod 16 and partner_instance[n, 1, i, k] = (n - L_i) mod 16 for a lag L_i in 1..15 that depends only on the axial plane i.
All inputs are finite; a program needn't handle non-finite values.
Results may differ from a plain program's by a relative error of at most 0.00005.
Values sent between devices are 32-bit elements; how exact they have to be, the bound alone decides.
No kernel may reach another device: no remote copies, remote signals or barrier semaphores. Data moves between devices by JAX's collectives and lax.ppermute only.
A program may use at most 64 MiB of HBM per device.

v0:
```python
import math
import jax
import jax.numpy as jnp
from jax import lax
from jax.sharding import PartitionSpec as P

SECTION_ALPHA = 0.5
PITCH_ANGLE = 2.0 * math.pi / 36.0
NYQUIST_DAMP = 2.0


def shifted(value, axis, by):
    devices = lax.axis_size(axis)
    return lax.ppermute(value, axis, [(i, (i + by) % devices) for i in range(devices)])


def extended_2(block, sides, width):
    for axis, dim in sides:
        count = lax.axis_size(axis)
        forward = [(i, i + 1) for i in range(count - 1)]
        backward = [(target, source) for source, target in forward]
        low = lax.ppermute(
            lax.slice_in_dim(block, block.shape[dim] - width, None, axis=dim), axis, forward
        )
        high = lax.ppermute(lax.slice_in_dim(block, 0, width, axis=dim), axis, backward)
        block = jnp.concatenate([low, block, high], axis=dim)
    return block


def time_weights(offset, count):
    offset = offset % count
    angle = math.pi * offset.astype(jnp.float32) / count
    parity = jnp.where(offset % 2 == 1, 1.0, -1.0).astype(jnp.float32)
    sine = jnp.where(offset == 0, 1.0, jnp.sin(angle))
    spectral = 0.5 * parity * jnp.cos(angle) / sine - NYQUIST_DAMP * parity / count
    return jnp.where(offset == 0, NYQUIST_DAMP / count, spectral)


def rotate_velocity(values, turn):
    cosine = math.cos(PITCH_ANGLE)
    sine = turn * math.sin(PITCH_ANGLE)
    second = values[:, 2]
    third = values[:, 3]
    return jnp.stack(
        [
            values[:, 0],
            values[:, 1],
            cosine * second - sine * third,
            sine * second + cosine * third,
            values[:, 4],
        ],
        axis=1,
    )


def section_update(
    state, base, pseudo_step, eddy_visc, jacobians, up_i, down_i, low_ghost, high_ghost, time_term
):
    up_j = jnp.concatenate([state[:, :, :, 1:], high_ghost[:, :, :, None]], axis=3)
    down_j = jnp.concatenate([low_ghost[:, :, :, None], state[:, :, :, :-1]], axis=3)
    zeros = jnp.zeros(state.shape[:4] + (1,), state.dtype)
    up_k = jnp.concatenate([state[..., 1:], zeros], axis=4)
    down_k = jnp.concatenate([zeros, state[..., :-1]], axis=4)
    diffs = jnp.stack([up_i - down_i, up_j - down_j, up_k - down_k], axis=0) * 0.5
    flux = jnp.einsum("dab,dnbijk->naijk", jacobians, diffs, precision=lax.Precision.HIGHEST)
    laplace = up_i + down_i + up_j + down_j + up_k + down_k - 6.0 * state
    spatial = flux - eddy_visc[None, None] * laplace
    return base - SECTION_ALPHA * pseudo_step[None, None] * (spatial + time_term)


def radial_table(partner_radial):
    radial_count = partner_radial.shape[2]
    radial_ids = jnp.arange(radial_count, dtype=jnp.int32)
    return (partner_radial[..., None] == radial_ids).astype(jnp.float32)


def per_device(state, base, pseudo_step, eddy_visc, jacobians, partner_radial, partner_instance):
    local_count = state.shape[0]
    cycle_size = lax.axis_size("tm")
    total_count = local_count * cycle_size
    position = lax.axis_index("tm")
    local_ids = jnp.arange(local_count, dtype=jnp.int32)
    own_ids = position * local_count + local_ids
    flattened = state.reshape(local_count, -1)
    start_weights = time_weights(own_ids[:, None] - own_ids[None, :], total_count)
    initial = jnp.dot(start_weights, flattened, precision=lax.Precision.HIGHEST)

    def one_turn(turn_index, carry):
        moving, accumulated = carry
        moving = shifted(moving, "tm", 1)
        anchor = (position - turn_index) % cycle_size
        source_ids = anchor * local_count + local_ids
        weights = time_weights(own_ids[:, None] - source_ids[None, :], total_count)
        return (moving, accumulated + jnp.dot(weights, moving, precision=lax.Precision.HIGHEST))

    moved_last, accumulated = lax.fori_loop(1, cycle_size, one_turn, (flattened, initial))
    time_term = accumulated.reshape(state.shape)
    radial_hot = radial_table(partner_radial)
    face_planes = jnp.stack([state[:, :, :, -1, :], state[:, :, :, 0, :]], axis=1)
    all_faces = lax.all_gather(face_planes, "tm", axis=0, tiled=True)
    instance_ids = jnp.arange(total_count, dtype=jnp.int32)
    instance_hot = (partner_instance[:, :, :, 0][..., None] == instance_ids).astype(jnp.float32)
    picked = jnp.einsum(
        "nsim,msvik->nsvik", instance_hot, all_faces, precision=lax.Precision.HIGHEST
    )
    remapped = jnp.einsum("nsvir,sikr->nsvik", picked, radial_hot, precision=lax.Precision.HIGHEST)
    low_ghost = rotate_velocity(remapped[:, 0], -1.0)
    high_ghost = rotate_velocity(remapped[:, 1], 1.0)
    extended = extended_2(state, (("space", 2),), 1)
    up_i = extended[:, :, 2:]
    down_i = extended[:, :, :-2]
    return section_update(
        state,
        base,
        pseudo_step,
        eddy_visc,
        jacobians,
        up_i,
        down_i,
        low_ghost,
        high_ghost,
        time_term,
    )


def solution(mesh):
    return jax.shard_map(
        per_device,
        mesh=mesh,
        in_specs=(
            P("tm", None, "space", None, None),
            P("tm", None, "space", None, None),
            P("space", None, None),
            P("space", None, None),
            P(),
            P(None, "space", None),
            P("tm", None, "space", None),
        ),
        out_specs=P("tm", None, "space", None, None),
        check_vma=False,
    )
```

profile of v0, /device:TPU:64, one launch (start us, length us, event | category | flops | bytes accessed | tf_op | source)
XLA Modules:
  0.0 639.7 jit_solution(3489502226336061569)
XLA Ops:
  7.9 75.3 %all_gather.3 = f32[16,2,5,8,128]{4,3,2,1,0:T(8,128)S(1)} all-gather(f32[1,2,5,8,128]{4,3,2,1,0:T(8,128)S(1)} %pad_maximum_fusion.4), channel_id=1, replica_groups=mesh['tm'=16,'space'=32] {'tm'}, dimensions={0}, use_global_device_ids=true | all-gather | bytes 696320 | tf_op jit(solution)/shard_map/all_gather | solution.py:100
  89.6 2.7 pad_subtract_fusion
  94.7 536.5 %while.18 = (s32[]{:T(128)}, f32[1,163840]{1,0:T(1,128)}, f32[1,163840]{1,0:T(1,128)S(1)}, s32[]{:T(128)}, s32[]{:T(128)}, /*index=5*/s32[]{:T(128)}, s32[]{:T(1...) while((s32[]{:T(128)}, f32[1,163840]{1,0:T(1,128)}, ...), condition=%wide.region_1.2_spmd, body=%wide.region_0.1_spmd.sunk | while | flops 327729 | bytes 5898953 | solution.py:96
  96.8 21.0 %collective-permute-done = f32[1,163840]{1,0:T(1,128)S(1)} collective-permute-done((f32[1,163840]{1,0:T(1,128)}, f32[1,163840]{1,0:T(1,128)S(1)}, u32[]{:S(2)}, u32[]{:S(2)}) %collective-permute-start) | collective-permute-done | bytes 655392 | tf_op jit(solution)/shard_map/while/body/eval_jaxpr/ppermute | solution.py:14
  121.6 25.5 %collective-permute-done = f32[1,163840]{1,0:T(1,128)S(1)} collective-permute-done((f32[1,163840]{1,0:T(1,128)}, f32[1,163840]{1,0:T(1,128)S(1)}, u32[]{:S(2)}, u32[]{:S(2)}) %collective-permute-start) | collective-permute-done | bytes 655392 | tf_op jit(solution)/shard_map/while/body/eval_jaxpr/ppermute | solution.py:14
  148.7 3.7 collective-permute-start
  152.6 24.9 %collective-permute-done = f32[1,163840]{1,0:T(1,128)S(1)} collective-permute-done((f32[1,163840]{1,0:T(1,128)}, f32[1,163840]{1,0:T(1,128)S(1)}, u32[]{:S(2)}, u32[]{:S(2)}) %collective-permute-start) | collective-permute-done | bytes 655392 | tf_op jit(solution)/shard_map/while/body/eval_jaxpr/ppermute | solution.py:14
  179.1 4.9 collective-permute-start
  184.2 19.7 %collective-permute-done = f32[1,163840]{1,0:T(1,128)S(1)} collective-permute-done((f32[1,163840]{1,0:T(1,128)}, f32[1,163840]{1,0:T(1,128)S(1)}, u32[]{:S(2)}, u32[]{:S(2)}) %collective-permute-start) | collective-permute-done | bytes 655392 | tf_op jit(solution)/shard_map/while/body/eval_jaxpr/ppermute | solution.py:14
  205.6 8.2 %collective-permute-start = (f32[1,163840]{1,0:T(1,128)}, f32[1,163840]{1,0:T(1,128)S(1)}, u32[]{:S(2)}, u32[]{:S(2)}) collective-permute-start(f32[1,163840]{1,0:T(1,128)} %get-tuple-element.213), channel_id=1, source_target_pairs={{0,32},{32,64},{64,96},{96,128},{128,160},{160,192},{192,224},{224... | collective-permute-start | bytes 1966088 | tf_op jit(solution)/shard_map/while/body/eval_jaxpr/ppermute | solution.py:14
  214.1 36.3 %collective-permute-done = f32[1,163840]{1,0:T(1,128)S(1)} collective-permute-done((f32[1,163840]{1,0:T(1,128)}, f32[1,163840]{1,0:T(1,128)S(1)}, u32[]{:S(2)}, u32[]{:S(2)}) %collective-permute-start) | collective-permute-done | bytes 655392 | tf_op jit(solution)/shard_map/while/body/eval_jaxpr/ppermute | solution.py:14
  254.1 27.1 %collective-permute-done = f32[1,163840]{1,0:T(1,128)S(1)} collective-permute-done((f32[1,163840]{1,0:T(1,128)}, f32[1,163840]{1,0:T(1,128)S(1)}, u32[]{:S(2)}, u32[]{:S(2)}) %collective-permute-start) | collective-permute-done | bytes 655392 | tf_op jit(solution)/shard_map/while/body/eval_jaxpr/ppermute | solution.py:14
  282.8 8.3 %collective-permute-start = (f32[1,163840]{1,0:T(1,128)}, f32[1,163840]{1,0:T(1,128)S(1)}, u32[]{:S(2)}, u32[]{:S(2)}) collective-permute-start(f32[1,163840]{1,0:T(1,128)} %get-tuple-element.213), channel_id=1, source_target_pairs={{0,32},{32,64},{64,96},{96,128},{128,160},{160,192},{192,224},{224... | collective-permute-start | bytes 1966088 | tf_op jit(solution)/shard_map/while/body/eval_jaxpr/ppermute | solution.py:14
  291.4 42.6 %collective-permute-done = f32[1,163840]{1,0:T(1,128)S(1)} collective-permute-done((f32[1,163840]{1,0:T(1,128)}, f32[1,163840]{1,0:T(1,128)S(1)}, u32[]{:S(2)}, u32[]{:S(2)}) %collective-permute-start) | collective-permute-done | bytes 655392 | tf_op jit(solution)/shard_map/while/body/eval_jaxpr/ppermute | solution.py:14
  337.8 37.0 %collective-permute-done = f32[1,163840]{1,0:T(1,128)S(1)} collective-permute-done((f32[1,163840]{1,0:T(1,128)}, f32[1,163840]{1,0:T(1,128)S(1)}, u32[]{:S(2)}, u32[]{:S(2)}) %collective-permute-start) | collective-permute-done | bytes 655392 | tf_op jit(solution)/shard_map/while/body/eval_jaxpr/ppermute | solution.py:14
  376.4 8.2 %collective-permute-start = (f32[1,163840]{1,0:T(1,128)}, f32[1,163840]{1,0:T(1,128)S(1)}, u32[]{:S(2)}, u32[]{:S(2)}) collective-permute-start(f32[1,163840]{1,0:T(1,128)} %get-tuple-element.213), channel_id=1, source_target_pairs={{0,32},{32,64},{64,96},{96,128},{128,160},{160,192},{192,224},{224... | collective-permute-start | bytes 1966088 | tf_op jit(solution)/shard_map/while/body/eval_jaxpr/ppermute | solution.py:14
  384.9 40.9 %collective-permute-done = f32[1,163840]{1,0:T(1,128)S(1)} collective-permute-done((f32[1,163840]{1,0:T(1,128)}, f32[1,163840]{1,0:T(1,128)S(1)}, u32[]{:S(2)}, u32[]{:S(2)}) %collective-permute-start) | collective-permute-done | bytes 655392 | tf_op jit(solution)/shard_map/while/body/eval_jaxpr/ppermute | solution.py:14
  429.6 35.7 %collective-permute-done = f32[1,163840]{1,0:T(1,128)S(1)} collective-permute-done((f32[1,163840]{1,0:T(1,128)}, f32[1,163840]{1,0:T(1,128)S(1)}, u32[]{:S(2)}, u32[]{:S(2)}) %collective-permute-start) | collective-permute-done | bytes 655392 | tf_op jit(solution)/shard_map/while/body/eval_jaxpr/ppermute | solution.py:14
  469.1 25.5 %collective-permute-done = f32[1,163840]{1,0:T(1,128)S(1)} collective-permute-done((f32[1,163840]{1,0:T(1,128)}, f32[1,163840]{1,0:T(1,128)S(1)}, u32[]{:S(2)}, u32[]{:S(2)}) %collective-permute-start) | collective-permute-done | bytes 655392 | tf_op jit(solution)/shard_map/while/body/eval_jaxpr/ppermute | solution.py:14
  498.4 36.0 %collective-permute-done = f32[1,163840]{1,0:T(1,128)S(1)} collective-permute-done((f32[1,163840]{1,0:T(1,128)}, f32[1,163840]{1,0:T(1,128)S(1)}, u32[]{:S(2)}, u32[]{:S(2)}) %collective-permute-start) | collective-permute-done | bytes 655392 | tf_op jit(solution)/shard_map/while/body/eval_jaxpr/ppermute | solution.py:14
  538.2 28.6 %collective-permute-done = f32[1,163840]{1,0:T(1,128)S(1)} collective-permute-done((f32[1,163840]{1,0:T(1,128)}, f32[1,163840]{1,0:T(1,128)S(1)}, u32[]{:S(2)}, u32[]{:S(2)}) %collective-permute-start) | collective-permute-done | bytes 655392 | tf_op jit(solution)/shard_map/while/body/eval_jaxpr/ppermute | solution.py:14
  570.5 35.1 %collective-permute-done = f32[1,163840]{1,0:T(1,128)S(1)} collective-permute-done((f32[1,163840]{1,0:T(1,128)}, f32[1,163840]{1,0:T(1,128)S(1)}, u32[]{:S(2)}, u32[]{:S(2)}) %collective-permute-start) | collective-permute-done | bytes 655392 | tf_op jit(solution)/shard_map/while/body/eval_jaxpr/ppermute | solution.py:14
  609.4 20.2 %collective-permute-done = f32[1,163840]{1,0:T(1,128)S(1)} collective-permute-done((f32[1,163840]{1,0:T(1,128)}, f32[1,163840]{1,0:T(1,128)S(1)}, u32[]{:S(2)}, u32[]{:S(2)}) %collective-permute-start) | collective-permute-done | bytes 655392 | tf_op jit(solution)/shard_map/while/body/eval_jaxpr/ppermute | solution.py:14
  631.2 7.5 %fusion.10 = f32[1,5,8,32,128]{4,1,0,3,2:T(8,128)S(1)} fusion(f32[1,5,8,32,128]{4,1,0,3,2:T(8,128)} %pad_subtract_fusion, f32[1,5,8,32,128]{4,1,0,3,2:T(8,128)} %fusion.12, f32[1,5,8,32,128]{4,1,0,3,2:T(8,128)} %fusion.13, f32[1,5,8,32,128]{4,3,2,1,0:T(8,128)} %param.10, f32[1,5,8,32,128]{4,3,2,1,0:T(8,128)S(1)} %bitcast.55, ...), kind=kOutput, calls=%fused_computation.12 | convolution fusion | flops 33587200 | bytes 7625004 | tf_op jit(solution)/shard_map/dab,dnbijk->naijk/dot_general | solution.py:65
  (87 shorter events, 60.4 us)
Async XLA Ops:
  0.0 631.2 %copy-start = (f32[3,5,5]{2,0,1:T(4,128)S(1)}, f32[3,5,5]{2,0,1:T(4,128)}, u32[]{:S(2)}) copy-start(f32[3,5,5]{2,0,1:T(4,128)} %param.13) | copy-start | bytes 904
  2.0 5.6 copy-start.7
  3.5 80.2 %copy-start.8 = (s32[2,8,128]{2,1,0:T(8,128)S(1)}, s32[2,8,128]{2,1,0:T(8,128)}, u32[]{:S(2)}) copy-start(s32[2,8,128]{2,1,0:T(8,128)} %param.14) | copy-start | bytes 24580
  3.5 90.0 %collective-permute-start.2 = (f32[1,5,1,32,128]{4,1,0,3,2:T(8,128)S(1)}, f32[1,5,1,32,128]{4,1,0,3,2:T(8,128)S(1)}, u32[]{:S(2)}, u32[]{:S(2)}) collective-permute-start(f32[1,5,1,32,128]{4,1,0,3,2:T(8,128)S(1)} %get-tuple-element.150), channel_id=1, source_target_pairs={{0,1},{1,2},{2,3},{3,4},{4,5},{5,6},{6,7},{7,8},{8,9},{9,10},{10,1... | collective-permute-start | bytes 245768 | tf_op jit(solution)/shard_map/ppermute | solution.py:22
  5.3 88.2 %collective-permute-start.1 = (f32[1,5,1,32,128]{4,1,0,3,2:T(8,128)S(1)}, f32[1,5,1,32,128]{4,1,0,3,2:T(8,128)S(1)}, u32[]{:S(2)}, u32[]{:S(2)}) collective-permute-start(f32[1,5,1,32,128]{4,1,0,3,2:T(8,128)S(1)} %get-tuple-element.151), channel_id=1, source_target_pairs={{1,0},{2,1},{3,2},{4,3},{5,4},{6,5},{7,6},{8,7},{9,8},{10,9},{11,1... | collective-permute-start | bytes 245768 | tf_op jit(solution)/shard_map/ppermute | solution.py:25
  89.6 2.8 copy-start.4
  89.6 2.7 copy-start.5
  89.6 2.7 copy-start.1
  89.6 2.7 copy-start.2
  94.7 23.2 %collective-permute-start = (f32[1,163840]{1,0:T(1,128)}, f32[1,163840]{1,0:T(1,128)S(1)}, u32[]{:S(2)}, u32[]{:S(2)}) collective-permute-start(f32[1,163840]{1,0:T(1,128)} %get-tuple-element.213), channel_id=1, source_target_pairs={{0,32},{32,64},{64,96},{96,128},{128,160},{160,192},{192,224},{224... | collective-permute-start | bytes 1966088 | tf_op jit(solution)/shard_map/while/body/eval_jaxpr/ppermute | solution.py:14
  119.5 27.7 %collective-permute-start = (f32[1,163840]{1,0:T(1,128)}, f32[1,163840]{1,0:T(1,128)S(1)}, u32[]{:S(2)}, u32[]{:S(2)}) collective-permute-start(f32[1,163840]{1,0:T(1,128)} %get-tuple-element.213), channel_id=1, source_target_pairs={{0,32},{32,64},{64,96},{96,128},{128,160},{160,192},{192,224},{224... | collective-permute-start | bytes 1966088 | tf_op jit(solution)/shard_map/while/body/eval_jaxpr/ppermute | solution.py:14
  148.7 28.8 %collective-permute-start = (f32[1,163840]{1,0:T(1,128)}, f32[1,163840]{1,0:T(1,128)S(1)}, u32[]{:S(2)}, u32[]{:S(2)}) collective-permute-start(f32[1,163840]{1,0:T(1,128)} %get-tuple-element.213), channel_id=1, source_target_pairs={{0,32},{32,64},{64,96},{96,128},{128,160},{160,192},{192,224},{224... | collective-permute-start | bytes 1966088 | tf_op jit(solution)/shard_map/while/body/eval_jaxpr/ppermute | solution.py:14
  179.1 24.9 %collective-permute-start = (f32[1,163840]{1,0:T(1,128)}, f32[1,163840]{1,0:T(1,128)S(1)}, u32[]{:S(2)}, u32[]{:S(2)}) collective-permute-start(f32[1,163840]{1,0:T(1,128)} %get-tuple-element.213), channel_id=1, source_target_pairs={{0,32},{32,64},{64,96},{96,128},{128,160},{160,192},{192,224},{224... | collective-permute-start | bytes 1966088 | tf_op jit(solution)/shard_map/while/body/eval_jaxpr/ppermute | solution.py:14
  205.6 44.8 %collective-permute-start = (f32[1,163840]{1,0:T(1,128)}, f32[1,163840]{1,0:T(1,128)S(1)}, u32[]{:S(2)}, u32[]{:S(2)}) collective-permute-start(f32[1,163840]{1,0:T(1,128)} %get-tuple-element.213), channel_id=1, source_target_pairs={{0,32},{32,64},{64,96},{96,128},{128,160},{160,192},{192,224},{224... | collective-permute-start | bytes 1966088 | tf_op jit(solution)/shard_map/while/body/eval_jaxpr/ppermute | solution.py:14
  251.9 29.3 %collective-permute-start = (f32[1,163840]{1,0:T(1,128)}, f32[1,163840]{1,0:T(1,128)S(1)}, u32[]{:S(2)}, u32[]{:S(2)}) collective-permute-start(f32[1,163840]{1,0:T(1,128)} %get-tuple-element.213), channel_id=1, source_target_pairs={{0,32},{32,64},{64,96},{96,128},{128,160},{160,192},{192,224},{224... | collective-permute-start | bytes 1966088 | tf_op jit(solution)/shard_map/while/body/eval_jaxpr/ppermute | solution.py:14
  282.8 51.2 %collective-permute-start = (f32[1,163840]{1,0:T(1,128)}, f32[1,163840]{1,0:T(1,128)S(1)}, u32[]{:S(2)}, u32[]{:S(2)}) collective-permute-start(f32[1,163840]{1,0:T(1,128)} %get-tuple-element.213), channel_id=1, source_target_pairs={{0,32},{32,64},{64,96},{96,128},{128,160},{160,192},{192,224},{224... | collective-permute-start | bytes 1966088 | tf_op jit(solution)/shard_map/while/body/eval_jaxpr/ppermute | solution.py:14
  335.6 39.2 %collective-permute-start = (f32[1,163840]{1,0:T(1,128)}, f32[1,163840]{1,0:T(1,128)S(1)}, u32[]{:S(2)}, u32[]{:S(2)}) collective-permute-start(f32[1,163840]{1,0:T(1,128)} %get-tuple-element.213), channel_id=1, source_target_pairs={{0,32},{32,64},{64,96},{96,128},{128,160},{160,192},{192,224},{224... | collective-permute-start | bytes 1966088 | tf_op jit(solution)/shard_map/while/body/eval_jaxpr/ppermute | solution.py:14
  376.4 49.4 %collective-permute-start = (f32[1,163840]{1,0:T(1,128)}, f32[1,163840]{1,0:T(1,128)S(1)}, u32[]{:S(2)}, u32[]{:S(2)}) collective-permute-start(f32[1,163840]{1,0:T(1,128)} %get-tuple-element.213), channel_id=1, source_target_pairs={{0,32},{32,64},{64,96},{96,128},{128,160},{160,192},{192,224},{224... | collective-permute-start | bytes 1966088 | tf_op jit(solution)/shard_map/while/body/eval_jaxpr/ppermute | solution.py:14
  427.5 37.9 %collective-permute-start = (f32[1,163840]{1,0:T(1,128)}, f32[1,163840]{1,0:T(1,128)S(1)}, u32[]{:S(2)}, u32[]{:S(2)}) collective-permute-start(f32[1,163840]{1,0:T(1,128)} %get-tuple-element.213), channel_id=1, source_target_pairs={{0,32},{32,64},{64,96},{96,128},{128,160},{160,192},{192,224},{224... | collective-permute-start | bytes 1966088 | tf_op jit(solution)/shard_map/while/body/eval_jaxpr/ppermute | solution.py:14
  467.0 27.6 %collective-permute-start = (f32[1,163840]{1,0:T(1,128)}, f32[1,163840]{1,0:T(1,128)S(1)}, u32[]{:S(2)}, u32[]{:S(2)}) collective-permute-start(f32[1,163840]{1,0:T(1,128)} %get-tuple-element.213), channel_id=1, source_target_pairs={{0,32},{32,64},{64,96},{96,128},{128,160},{160,192},{192,224},{224... | collective-permute-start | bytes 1966088 | tf_op jit(solution)/shard_map/while/body/eval_jaxpr/ppermute | solution.py:14
  496.2 38.2 %collective-permute-start = (f32[1,163840]{1,0:T(1,128)}, f32[1,163840]{1,0:T(1,128)S(1)}, u32[]{:S(2)}, u32[]{:S(2)}) collective-permute-start(f32[1,163840]{1,0:T(1,128)} %get-tuple-element.213), channel_id=1, source_target_pairs={{0,32},{32,64},{64,96},{96,128},{128,160},{160,192},{192,224},{224... | collective-permute-start | bytes 1966088 | tf_op jit(solution)/shard_map/while/body/eval_jaxpr/ppermute | solution.py:14
  536.0 30.7 %collective-permute-start = (f32[1,163840]{1,0:T(1,128)}, f32[1,163840]{1,0:T(1,128)S(1)}, u32[]{:S(2)}, u32[]{:S(2)}) collective-permute-start(f32[1,163840]{1,0:T(1,128)} %get-tuple-element.213), channel_id=1, source_target_pairs={{0,32},{32,64},{64,96},{96,128},{128,160},{160,192},{192,224},{224... | collective-permute-start | bytes 1966088 | tf_op jit(solution)/shard_map/while/body/eval_jaxpr/ppermute | solution.py:14
  568.4 37.2 %collective-permute-start = (f32[1,163840]{1,0:T(1,128)}, f32[1,163840]{1,0:T(1,128)S(1)}, u32[]{:S(2)}, u32[]{:S(2)}) collective-permute-start(f32[1,163840]{1,0:T(1,128)} %get-tuple-element.213), channel_id=1, source_target_pairs={{0,32},{32,64},{64,96},{96,128},{128,160},{160,192},{192,224},{224... | collective-permute-start | bytes 1966088 | tf_op jit(solution)/shard_map/while/body/eval_jaxpr/ppermute | solution.py:14
  607.2 22.4 %collective-permute-start = (f32[1,163840]{1,0:T(1,128)}, f32[1,163840]{1,0:T(1,128)S(1)}, u32[]{:S(2)}, u32[]{:S(2)}) collective-permute-start(f32[1,163840]{1,0:T(1,128)} %get-tuple-element.213), channel_id=1, source_target_pairs={{0,32},{32,64},{64,96},{96,128},{128,160},{160,192},{192,224},{224... | collective-permute-start | bytes 1966088 | tf_op jit(solution)/shard_map/while/body/eval_jaxpr/ppermute | solution.py:14
  (2 other events, 2.5 us)
where the time goes:
time: 640 us
  waiting for transfers between devices  456 us (71%)
  blocking collectives  75.3 us (12%)
  starting transfers between devices  55.5 us (9%)
  local copies, waits for them, and re-layouts  21 us (3%)
  other arithmetic  18.1 us (3%)
  matrix products  9.23 us (1%)
    ppermute x15, waiting for transfers between devices, shifted(): lax.ppermute(value, axis, [(i, (i + by) % devices) for i in range(devices)])  456 us
    all_gather x1, blocking collectives, per_device(): all_faces = lax.all_gather(face_planes, 'tm', axis=0, tiled=True)  75.3 us
    ppermute x15, starting transfers between devices, shifted(): lax.ppermute(value, axis, [(i, (i + by) % devices) for i in range(devices)])  52.5 us
  transfers between devices with their start and end apart: 17, of which 15 were waited for; matrix products, arithmetic and copies ran while one was open for 2% of the time, Pallas kernels for 0%

commit v1 on v0

--- a/solution.py
+++ b/solution.py
@@ -97,7 +97,8 @@
     time_term = accumulated.reshape(state.shape)
     radial_hot = radial_table(partner_radial)
     face_planes = jnp.stack([state[:, :, :, -1, :], state[:, :, :, 0, :]], axis=1)
-    all_faces = lax.all_gather(face_planes, "tm", axis=0, tiled=True)
+    repeated = jnp.stack([face_planes] * lax.axis_size("tm"))
+    all_faces = jnp.concatenate(lax.all_to_all(repeated, "tm", 0, 0), axis=0)
     instance_ids = jnp.arange(total_count, dtype=jnp.int32)
     instance_hot = (partner_instance[:, :, :, 0][..., None] == instance_ids).astype(jnp.float32)
     picked = jnp.einsum(

time: 640 us -> 603 us (0.942)
  the two profiles are of different devices: /device:TPU:64 before, /device:TPU:184 now
where the time goes in v1:
time: 603 us; the launch traced here: 602 us
  waiting for transfers between devices  384 us (64%)
  starting transfers between devices  167 us (28%)
  local copies, waits for them, and re-layouts  18.7 us (3%)
  other arithmetic  17.8 us (3%)
  matrix products  9.91 us (2%)
    ppermute x15, waiting for transfers between devices, shifted(): lax.ppermute(value, axis, [(i, (i + by) % devices) for i in range(devices)])  373 us
    ppermute x15, starting transfers between devices, shifted(): lax.ppermute(value, axis, [(i, (i + by) % devices) for i in range(devices)])  148 us
    all_to_all x1, starting transfers between devices, per_device(): all_faces = jnp.concatenate(lax.all_to_all(repeated, 'tm', 0, 0), axis=0)  13.9 us
    while x15, local copies, waits for them, and re-layouts  12.5 us
  transfers between devices with their start and end apart: 18, of which 17 were waited for; matrix products, arithmetic and copies ran while one was open for 1% of the time, Pallas kernels for 0%

profile of v1, /device:TPU:184, one launch (start us, length us, event | category | flops | bytes accessed | tf_op | source)
XLA Modules:
  0.0 602.2 jit_solution(88207624544019652)
XLA Ops:
  2.1 13.9 %all-to-all-start = ((f32[16,1,2,5,8,128]{5,4,3,2,1,0:T(8,128)}), f32[16,1,2,5,8,128]{5,4,3,2,1,0:T(8,128)S(1)}, u32[]{:S(2)}, u32[]{:S(2)}) async-start(f32[16,1,2,5,8,128]{5,4,3,2,1,0:T(8,128)} %stack.16), calls=%async_computation | async-start | bytes 1310720 | tf_op jit(solution)/shard_map/all_to_all | solution.py:101
  44.7 549.0 %while.18 = (s32[]{:T(128)}, f32[1,163840]{1,0:T(1,128)}, f32[1,163840]{1,0:T(1,128)S(1)}, s32[]{:T(128)}, s32[]{:T(128)}, /*index=5*/s32[]{:T(128)}, s32[]{:T(1...) while((s32[]{:T(128)}, f32[1,163840]{1,0:T(1,128)}, ...), condition=%wide.region_1.2_spmd, body=%wide.region_0.1_spmd.sunk | while | flops 327729 | bytes 5898953 | solution.py:96
  46.9 34.5 %collective-permute-done = f32[1,163840]{1,0:T(1,128)S(1)} collective-permute-done((f32[1,163840]{1,0:T(1,128)}, f32[1,163840]{1,0:T(1,128)S(1)}, u32[]{:S(2)}, u32[]{:S(2)}) %collective-permute-start) | collective-permute-done | bytes 655392 | tf_op jit(solution)/shard_map/while/body/eval_jaxpr/ppermute | solution.py:14
  85.1 16.0 %collective-permute-done = f32[1,163840]{1,0:T(1,128)S(1)} collective-permute-done((f32[1,163840]{1,0:T(1,128)}, f32[1,163840]{1,0:T(1,128)S(1)}, u32[]{:S(2)}, u32[]{:S(2)}) %collective-permute-start) | collective-permute-done | bytes 655392 | tf_op jit(solution)/shard_map/while/body/eval_jaxpr/ppermute | solution.py:14
  106.5 21.6 %collective-permute-done = f32[1,163840]{1,0:T(1,128)S(1)} collective-permute-done((f32[1,163840]{1,0:T(1,128)}, f32[1,163840]{1,0:T(1,128)S(1)}, u32[]{:S(2)}, u32[]{:S(2)}) %collective-permute-start) | collective-permute-done | bytes 655392 | tf_op jit(solution)/shard_map/while/body/eval_jaxpr/ppermute | solution.py:14
  129.7 25.1 %collective-permute-start = (f32[1,163840]{1,0:T(1,128)}, f32[1,163840]{1,0:T(1,128)S(1)}, u32[]{:S(2)}, u32[]{:S(2)}) collective-permute-start(f32[1,163840]{1,0:T(1,128)} %get-tuple-element.213), channel_id=1, source_target_pairs={{0,32},{32,64},{64,96},{96,128},{128,160},{160,192},{192,224},{224... | collective-permute-start | bytes 1966088 | tf_op jit(solution)/shard_map/while/body/eval_jaxpr/ppermute | solution.py:14
  155.1 26.9 %collective-permute-done = f32[1,163840]{1,0:T(1,128)S(1)} collective-permute-done((f32[1,163840]{1,0:T(1,128)}, f32[1,163840]{1,0:T(1,128)S(1)}, u32[]{:S(2)}, u32[]{:S(2)}) %collective-permute-start) | collective-permute-done | bytes 655392 | tf_op jit(solution)/shard_map/while/body/eval_jaxpr/ppermute | solution.py:14
  183.6 25.5 %collective-permute-start = (f32[1,163840]{1,0:T(1,128)}, f32[1,163840]{1,0:T(1,128)S(1)}, u32[]{:S(2)}, u32[]{:S(2)}) collective-permute-start(f32[1,163840]{1,0:T(1,128)} %get-tuple-element.213), channel_id=1, source_target_pairs={{0,32},{32,64},{64,96},{96,128},{128,160},{160,192},{192,224},{224... | collective-permute-start | bytes 1966088 | tf_op jit(solution)/shard_map/while/body/eval_jaxpr/ppermute | solution.py:14
  209.3 27.2 %collective-permute-done = f32[1,163840]{1,0:T(1,128)S(1)} collective-permute-done((f32[1,163840]{1,0:T(1,128)}, f32[1,163840]{1,0:T(1,128)S(1)}, u32[]{:S(2)}, u32[]{:S(2)}) %collective-permute-start) | collective-permute-done | bytes 655392 | tf_op jit(solution)/shard_map/while/body/eval_jaxpr/ppermute | solution.py:14
  238.1 11.9 %collective-permute-start = (f32[1,163840]{1,0:T(1,128)}, f32[1,163840]{1,0:T(1,128)S(1)}, u32[]{:S(2)}, u32[]{:S(2)}) collective-permute-start(f32[1,163840]{1,0:T(1,128)} %get-tuple-element.213), channel_id=1, source_target_pairs={{0,32},{32,64},{64,96},{96,128},{128,160},{160,192},{192,224},{224... | collective-permute-start | bytes 1966088 | tf_op jit(solution)/shard_map/while/body/eval_jaxpr/ppermute | solution.py:14
  250.3 21.6 %collective-permute-done = f32[1,163840]{1,0:T(1,128)S(1)} collective-permute-done((f32[1,163840]{1,0:T(1,128)}, f32[1,163840]{1,0:T(1,128)S(1)}, u32[]{:S(2)}, u32[]{:S(2)}) %collective-permute-start) | collective-permute-done | bytes 655392 | tf_op jit(solution)/shard_map/while/body/eval_jaxpr/ppermute | solution.py:14
  273.5 29.1 %collective-permute-start = (f32[1,163840]{1,0:T(1,128)}, f32[1,163840]{1,0:T(1,128)S(1)}, u32[]{:S(2)}, u32[]{:S(2)}) collective-permute-start(f32[1,163840]{1,0:T(1,128)} %get-tuple-element.213), channel_id=1, source_target_pairs={{0,32},{32,64},{64,96},{96,128},{128,160},{160,192},{192,224},{224... | collective-permute-start | bytes 1966088 | tf_op jit(solution)/shard_map/while/body/eval_jaxpr/ppermute | solution.py:14
  302.9 31.5 %collective-permute-done = f32[1,163840]{1,0:T(1,128)S(1)} collective-permute-done((f32[1,163840]{1,0:T(1,128)}, f32[1,163840]{1,0:T(1,128)S(1)}, u32[]{:S(2)}, u32[]{:S(2)}) %collective-permute-start) | collective-permute-done | bytes 655392 | tf_op jit(solution)/shard_map/while/body/eval_jaxpr/ppermute | solution.py:14
  336.0 9.1 %collective-permute-start = (f32[1,163840]{1,0:T(1,128)}, f32[1,163840]{1,0:T(1,128)S(1)}, u32[]{:S(2)}, u32[]{:S(2)}) collective-permute-start(f32[1,163840]{1,0:T(1,128)} %get-tuple-element.213), channel_id=1, source_target_pairs={{0,32},{32,64},{64,96},{96,128},{128,160},{160,192},{192,224},{224... | collective-permute-start | bytes 1966088 | tf_op jit(solution)/shard_map/while/body/eval_jaxpr/ppermute | solution.py:14
  345.4 24.8 %collective-permute-done = f32[1,163840]{1,0:T(1,128)S(1)} collective-permute-done((f32[1,163840]{1,0:T(1,128)}, f32[1,163840]{1,0:T(1,128)S(1)}, u32[]{:S(2)}, u32[]{:S(2)}) %collective-permute-start) | collective-permute-done | bytes 655392 | tf_op jit(solution)/shard_map/while/body/eval_jaxpr/ppermute | solution.py:14
  371.8 8.3 %collective-permute-start = (f32[1,163840]{1,0:T(1,128)}, f32[1,163840]{1,0:T(1,128)S(1)}, u32[]{:S(2)}, u32[]{:S(2)}) collective-permute-start(f32[1,163840]{1,0:T(1,128)} %get-tuple-element.213), channel_id=1, source_target_pairs={{0,32},{32,64},{64,96},{96,128},{128,160},{160,192},{192,224},{224... | collective-permute-start | bytes 1966088 | tf_op jit(solution)/shard_map/while/body/eval_jaxpr/ppermute | solution.py:14
  380.4 23.0 %collective-permute-done = f32[1,163840]{1,0:T(1,128)S(1)} collective-permute-done((f32[1,163840]{1,0:T(1,128)}, f32[1,163840]{1,0:T(1,128)S(1)}, u32[]{:S(2)}, u32[]{:S(2)}) %collective-permute-start) | collective-permute-done | bytes 655392 | tf_op jit(solution)/shard_map/while/body/eval_jaxpr/ppermute | solution.py:14
  412.6 37.3 %collective-permute-done = f32[1,163840]{1,0:T(1,128)S(1)} collective-permute-done((f32[1,163840]{1,0:T(1,128)}, f32[1,163840]{1,0:T(1,128)S(1)}, u32[]{:S(2)}, u32[]{:S(2)}) %collective-permute-start) | collective-permute-done | bytes 655392 | tf_op jit(solution)/shard_map/while/body/eval_jaxpr/ppermute | solution.py:14
  453.8 29.5 %collective-permute-done = f32[1,163840]{1,0:T(1,128)S(1)} collective-permute-done((f32[1,163840]{1,0:T(1,128)}, f32[1,163840]{1,0:T(1,128)S(1)}, u32[]{:S(2)}, u32[]{:S(2)}) %collective-permute-start) | collective-permute-done | bytes 655392 | tf_op jit(solution)/shard_map/while/body/eval_jaxpr/ppermute | solution.py:14
  488.5 31.4 %collective-permute-done = f32[1,163840]{1,0:T(1,128)S(1)} collective-permute-done((f32[1,163840]{1,0:T(1,128)}, f32[1,163840]{1,0:T(1,128)S(1)}, u32[]{:S(2)}, u32[]{:S(2)}) %collective-permute-start) | collective-permute-done | bytes 655392 | tf_op jit(solution)/shard_map/while/body/eval_jaxpr/ppermute | solution.py:14
  526.8 16.6 %collective-permute-done = f32[1,163840]{1,0:T(1,128)S(1)} collective-permute-done((f32[1,163840]{1,0:T(1,128)}, f32[1,163840]{1,0:T(1,128)S(1)}, u32[]{:S(2)}, u32[]{:S(2)}) %collective-permute-start) | collective-permute-done | bytes 655392 | tf_op jit(solution)/shard_map/while/body/eval_jaxpr/ppermute | solution.py:14
  552.5 15.7 %collective-permute-done = f32[1,163840]{1,0:T(1,128)S(1)} collective-permute-done((f32[1,163840]{1,0:T(1,128)}, f32[1,163840]{1,0:T(1,128)S(1)}, u32[]{:S(2)}, u32[]{:S(2)}) %collective-permute-start) | collective-permute-done | bytes 655392 | tf_op jit(solution)/shard_map/while/body/eval_jaxpr/ppermute | solution.py:14
  576.6 15.5 %collective-permute-done = f32[1,163840]{1,0:T(1,128)S(1)} collective-permute-done((f32[1,163840]{1,0:T(1,128)}, f32[1,163840]{1,0:T(1,128)S(1)}, u32[]{:S(2)}, u32[]{:S(2)}) %collective-permute-start) | collective-permute-done | bytes 655392 | tf_op jit(solution)/shard_map/while/body/eval_jaxpr/ppermute | solution.py:14
  593.7 7.5 %fusion.10 = f32[1,5,8,32,128]{4,1,0,3,2:T(8,128)S(1)} fusion(f32[1,5,8,32,128]{4,1,0,3,2:T(8,128)} %pad_subtract_fusion, f32[1,5,8,32,128]{4,1,0,3,2:T(8,128)} %fusion.12, f32[1,5,8,32,128]{4,1,0,3,2:T(8,128)} %fusion.13, f32[1,5,8,32,128]{4,3,2,1,0:T(8,128)} %param.10, f32[1,5,8,32,128]{4,3,2,1,0:T(8,128)S(1)} %bitcast.56, ...), kind=kOutput, calls=%fused_computation.12 | convolution fusion | flops 33587200 | bytes 7625004 | tf_op jit(solution)/shard_map/dab,dnbijk->naijk/dot_general | solution.py:65
  (87 shorter events, 94.1 us)
Async XLA Ops:
  0.0 593.7 %copy-start = (f32[3,5,5]{2,0,1:T(4,128)S(1)}, f32[3,5,5]{2,0,1:T(4,128)}, u32[]{:S(2)}) copy-start(f32[3,5,5]{2,0,1:T(4,128)} %param.13) | copy-start | bytes 904
  1.1 22.5 %copy-start.3 = (f32[1,5,8,32,128]{4,3,2,1,0:T(8,128)}, f32[1,5,8,32,128]{4,3,2,1,0:T(8,128)S(1)}, u32[]{:S(2)}) copy-start(f32[1,5,8,32,128]{4,3,2,1,0:T(8,128)S(1)} %copy.87) | copy-start | bytes 1966084
  2.1 37.6 %all-to-all-start = ((f32[16,1,2,5,8,128]{5,4,3,2,1,0:T(8,128)}), f32[16,1,2,5,8,128]{5,4,3,2,1,0:T(8,128)S(1)}, u32[]{:S(2)}, u32[]{:S(2)}) async-start(f32[16,1,2,5,8,128]{5,4,3,2,1,0:T(8,128)} %stack.16), calls=%async_computation | async-start | bytes 1310720 | tf_op jit(solution)/shard_map/all_to_all | solution.py:101
  16.0 6.7 %copy-start.7 = (s32[1,2,8,128]{3,2,1,0:T(8,128)S(1)}, s32[1,2,8,128]{3,2,1,0:T(8,128)}, u32[]{:S(2)}) copy-start(s32[1,2,8,128]{3,2,1,0:T(8,128)} %param.15) | copy-start | bytes 24580
  16.0 6.9 %copy-start.6 = (f32[8,32,128]{2,1,0:T(8,128)S(1)}, f32[8,32,128]{2,1,0:T(8,128)}, u32[]{:S(2)}) copy-start(f32[8,32,128]{2,1,0:T(8,128)} %param.11) | copy-start | bytes 393220
  17.2 15.8 %collective-permute-start.2 = (f32[1,5,1,32,128]{4,1,0,3,2:T(8,128)}, f32[1,5,1,32,128]{4,1,0,3,2:T(8,128)S(1)}, u32[]{:S(2)}, u32[]{:S(2)}) collective-permute-start(f32[1,5,1,32,128]{4,1,0,3,2:T(8,128)} %get-tuple-element.150), channel_id=1, source_target_pairs={{0,1},{1,2},{2,3},{3,4},{4,5},{5,6},{6,7},{7,8},{8,9},{9,10},{10,1... | collective-permute-start | bytes 245768 | tf_op jit(solution)/shard_map/ppermute | solution.py:22
  19.1 18.6 %collective-permute-start.1 = (f32[1,5,1,32,128]{4,1,0,3,2:T(8,128)}, f32[1,5,1,32,128]{4,1,0,3,2:T(8,128)}, u32[]{:S(2)}, u32[]{:S(2)}) collective-permute-start(f32[1,5,1,32,128]{4,1,0,3,2:T(8,128)} %get-tuple-element.151), channel_id=1, source_target_pairs={{1,0},{2,1},{3,2},{4,3},{5,4},{6,5},{7,6},{8,7},{9,8},{10,9},{11,1... | collective-permute-start | bytes 245768 | tf_op jit(solution)/shard_map/ppermute | solution.py:25
  39.7 2.6 copy-start.2
  42.2 2.4 copy-start.4
  44.7 36.6 %collective-permute-start = (f32[1,163840]{1,0:T(1,128)}, f32[1,163840]{1,0:T(1,128)S(1)}, u32[]{:S(2)}, u32[]{:S(2)}) collective-permute-start(f32[1,163840]{1,0:T(1,128)} %get-tuple-element.213), channel_id=1, source_target_pairs={{0,32},{32,64},{64,96},{96,128},{128,160},{160,192},{192,224},{224... | collective-permute-start | bytes 1966088 | tf_op jit(solution)/shard_map/while/body/eval_jaxpr/ppermute | solution.py:14
  82.9 18.1 %collective-permute-start = (f32[1,163840]{1,0:T(1,128)}, f32[1,163840]{1,0:T(1,128)S(1)}, u32[]{:S(2)}, u32[]{:S(2)}) collective-permute-start(f32[1,163840]{1,0:T(1,128)} %get-tuple-element.213), channel_id=1, source_target_pairs={{0,32},{32,64},{64,96},{96,128},{128,160},{160,192},{192,224},{224... | collective-permute-start | bytes 1966088 | tf_op jit(solution)/shard_map/while/body/eval_jaxpr/ppermute | solution.py:14
  102.6 25.5 %collective-permute-start = (f32[1,163840]{1,0:T(1,128)}, f32[1,163840]{1,0:T(1,128)S(1)}, u32[]{:S(2)}, u32[]{:S(2)}) collective-permute-start(f32[1,163840]{1,0:T(1,128)} %get-tuple-element.213), channel_id=1, source_target_pairs={{0,32},{32,64},{64,96},{96,128},{128,160},{160,192},{192,224},{224... | collective-permute-start | bytes 1966088 | tf_op jit(solution)/shard_map/while/body/eval_jaxpr/ppermute | solution.py:14
  129.7 52.3 %collective-permute-start = (f32[1,163840]{1,0:T(1,128)}, f32[1,163840]{1,0:T(1,128)S(1)}, u32[]{:S(2)}, u32[]{:S(2)}) collective-permute-start(f32[1,163840]{1,0:T(1,128)} %get-tuple-element.213), channel_id=1, source_target_pairs={{0,32},{32,64},{64,96},{96,128},{128,160},{160,192},{192,224},{224... | collective-permute-start | bytes 1966088 | tf_op jit(solution)/shard_map/while/body/eval_jaxpr/ppermute | solution.py:14
  183.6 52.9 %collective-permute-start = (f32[1,163840]{1,0:T(1,128)}, f32[1,163840]{1,0:T(1,128)S(1)}, u32[]{:S(2)}, u32[]{:S(2)}) collective-permute-start(f32[1,163840]{1,0:T(1,128)} %get-tuple-element.213), channel_id=1, source_target_pairs={{0,32},{32,64},{64,96},{96,128},{128,160},{160,192},{192,224},{224... | collective-permute-start | bytes 1966088 | tf_op jit(solution)/shard_map/while/body/eval_jaxpr/ppermute | solution.py:14
  238.1 33.8 %collective-permute-start = (f32[1,163840]{1,0:T(1,128)}, f32[1,163840]{1,0:T(1,128)S(1)}, u32[]{:S(2)}, u32[]{:S(2)}) collective-permute-start(f32[1,163840]{1,0:T(1,128)} %get-tuple-element.213), channel_id=1, source_target_pairs={{0,32},{32,64},{64,96},{96,128},{128,160},{160,192},{192,224},{224... | collective-permute-start | bytes 1966088 | tf_op jit(solution)/shard_map/while/body/eval_jaxpr/ppermute | solution.py:14
  273.5 60.9 %collective-permute-start = (f32[1,163840]{1,0:T(1,128)}, f32[1,163840]{1,0:T(1,128)S(1)}, u32[]{:S(2)}, u32[]{:S(2)}) collective-permute-start(f32[1,163840]{1,0:T(1,128)} %get-tuple-element.213), channel_id=1, source_target_pairs={{0,32},{32,64},{64,96},{96,128},{128,160},{160,192},{192,224},{224... | collective-permute-start | bytes 1966088 | tf_op jit(solution)/shard_map/while/body/eval_jaxpr/ppermute | solution.py:14
  336.0 34.2 %collective-permute-start = (f32[1,163840]{1,0:T(1,128)}, f32[1,163840]{1,0:T(1,128)S(1)}, u32[]{:S(2)}, u32[]{:S(2)}) collective-permute-start(f32[1,163840]{1,0:T(1,128)} %get-tuple-element.213), channel_id=1, source_target_pairs={{0,32},{32,64},{64,96},{96,128},{128,160},{160,192},{192,224},{224... | collective-permute-start | bytes 1966088 | tf_op jit(solution)/shard_map/while/body/eval_jaxpr/ppermute | solution.py:14
  371.8 31.6 %collective-permute-start = (f32[1,163840]{1,0:T(1,128)}, f32[1,163840]{1,0:T(1,128)S(1)}, u32[]{:S(2)}, u32[]{:S(2)}) collective-permute-start(f32[1,163840]{1,0:T(1,128)} %get-tuple-element.213), channel_id=1, source_target_pairs={{0,32},{32,64},{64,96},{96,128},{128,160},{160,192},{192,224},{224... | collective-permute-start | bytes 1966088 | tf_op jit(solution)/shard_map/while/body/eval_jaxpr/ppermute | solution.py:14
  405.0 44.9 %collective-permute-start = (f32[1,163840]{1,0:T(1,128)}, f32[1,163840]{1,0:T(1,128)S(1)}, u32[]{:S(2)}, u32[]{:S(2)}) collective-permute-start(f32[1,163840]{1,0:T(1,128)} %get-tuple-element.213), channel_id=1, source_target_pairs={{0,32},{32,64},{64,96},{96,128},{128,160},{160,192},{192,224},{224... | collective-permute-start | bytes 1966088 | tf_op jit(solution)/shard_map/while/body/eval_jaxpr/ppermute | solution.py:14
  451.6 31.7 %collective-permute-start = (f32[1,163840]{1,0:T(1,128)}, f32[1,163840]{1,0:T(1,128)S(1)}, u32[]{:S(2)}, u32[]{:S(2)}) collective-permute-start(f32[1,163840]{1,0:T(1,128)} %get-tuple-element.213), channel_id=1, source_target_pairs={{0,32},{32,64},{64,96},{96,128},{128,160},{160,192},{192,224},{224... | collective-permute-start | bytes 1966088 | tf_op jit(solution)/shard_map/while/body/eval_jaxpr/ppermute | solution.py:14
  484.9 35.0 %collective-permute-start = (f32[1,163840]{1,0:T(1,128)}, f32[1,163840]{1,0:T(1,128)S(1)}, u32[]{:S(2)}, u32[]{:S(2)}) collective-permute-start(f32[1,163840]{1,0:T(1,128)} %get-tuple-element.213), channel_id=1, source_target_pairs={{0,32},{32,64},{64,96},{96,128},{128,160},{160,192},{192,224},{224... | collective-permute-start | bytes 1966088 | tf_op jit(solution)/shard_map/while/body/eval_jaxpr/ppermute | solution.py:14
  521.5 21.9 %collective-permute-start = (f32[1,163840]{1,0:T(1,128)}, f32[1,163840]{1,0:T(1,128)S(1)}, u32[]{:S(2)}, u32[]{:S(2)}) collective-permute-start(f32[1,163840]{1,0:T(1,128)} %get-tuple-element.213), channel_id=1, source_target_pairs={{0,32},{32,64},{64,96},{96,128},{128,160},{160,192},{192,224},{224... | collective-permute-start | bytes 1966088 | tf_op jit(solution)/shard_map/while/body/eval_jaxpr/ppermute | solution.py:14
  545.0 23.2 %collective-permute-start = (f32[1,163840]{1,0:T(1,128)}, f32[1,163840]{1,0:T(1,128)S(1)}, u32[]{:S(2)}, u32[]{:S(2)}) collective-permute-start(f32[1,163840]{1,0:T(1,128)} %get-tuple-element.213), channel_id=1, source_target_pairs={{0,32},{32,64},{64,96},{96,128},{128,160},{160,192},{192,224},{224... | collective-permute-start | bytes 1966088 | tf_op jit(solution)/shard_map/while/body/eval_jaxpr/ppermute | solution.py:14
  569.8 22.3 %collective-permute-start = (f32[1,163840]{1,0:T(1,128)}, f32[1,163840]{1,0:T(1,128)S(1)}, u32[]{:S(2)}, u32[]{:S(2)}) collective-permute-start(f32[1,163840]{1,0:T(1,128)} %get-tuple-element.213), channel_id=1, source_target_pairs={{0,32},{32,64},{64,96},{96,128},{128,160},{160,192},{192,224},{224... | collective-permute-start | bytes 1966088 | tf_op jit(solution)/shard_map/while/body/eval_jaxpr/ppermute | solution.py:14
  (2 other events, 3.8 us)
